TPU v7x, 512 devices: a whole 4x4x16 slice. The times are simulated.
512 devices in a mesh: dp: 4 (over x), tensor: 128 (over y, z, core).
Axes of the slice: x: 4, y: 4, z: 16, core: 2. Of those that a mesh axis runs over, the one named last changes fastest.
Arguments:
- stream: bfloat16 [32768, 2560], P(('dp', 'tensor')), parts along dimension 0, may hold values from -6 to 6
- queries: bfloat16 [512, 2560], P(('dp', 'tensor')), parts along dimension 0, may hold values from -170 to 170
- fresh_entries: bfloat16 [512, 1024], P(('dp', 'tensor')), parts along dimension 0, may hold values from -6 to 6
- paged_store_cache: bfloat16 [2560, 2, 128, 512], P(('dp', 'tensor')), parts along dimension 0, may hold values from -6 to 6
- page_table: int32 [512, 32], P('dp'), parts along dimension 0, may hold values from -1 to 639, as said below
- cache_length: int32 [512], P('dp'), parts along dimension 0, may hold values from 1 to 4096, as said below
- out_proj: bfloat16 [2560, 2560], P(None, 'tensor'), may hold values from -0.125 to 0.125
- norm_gain: bfloat16 [2560], replicated, may hold values from 0.099609375 to 1.8984375
- router: bfloat16 [2560, 64], replicated, may hold values from -0.125 to 0.125
- routes: int32 [32768, 6], P(('dp', 'tensor')), parts along dimension 0, may hold values from 0 to 63, as said below
- gate_up: bfloat16 [2, 24576, 2560], P(None, 'tensor'), may hold values from -0.125 to 0.125
- down_proj: bfloat16 [24576, 2560], P('tensor'), may hold values from -0.15625 to 0.15625
Outputs:
- layer_out: bfloat16 [32768, 2560], P(('dp', 'tensor')), parts along dimension 0
There are 4 independent parts, one for each index of `dp`. A program takes and returns all parts, laid end to end along the dimension named above; an argument that names none is the same for every part. Nothing has to cross between parts.
Inputs may be any that keep to these rules, and one draw needn't show every extreme that they name: `routes`: each row names 6 different experts. The rows of one device name each expert at most 6 times, and on every device one and the same expert below 16 is named exactly 6 times. `page_table`: row r lists in order the pages of request r's cache, ceil(cache_length[r] / 128) of them, then -1; every page belongs to exactly one request. `cache_length`: some request's cache holds exactly 4096 tokens.
All inputs are finite; a program needn't handle non-finite values.
Results may differ from a plain program's by a relative error of at most 0.0045.
Values may be sent and summed in bfloat16 or wider, within the bound.
No kernel may reach another device: no remote copies, remote signals or barrier semaphores. Data moves between devices by JAX's collectives and lax.ppermute only.
A program may use at most 64 MiB of HBM per device.

v0:
```python
import math
import jax
import jax.numpy as jnp
from jax import lax
from jax.sharding import PartitionSpec as P

QUERY_HEADS = 20
KEY_VALUE_HEADS = 4
HEAD_SIZE = 128
GROUP = 8
CAP = 6
NEG_FILL = -1e30
EPSILON = 1e-05


def finish_context(maxima, totals, accum, local_queries, local_entries):
    entry_count = local_queries.shape[0]
    key_value_width = KEY_VALUE_HEADS * HEAD_SIZE
    query_vector = local_queries.reshape(
        entry_count, KEY_VALUE_HEADS, QUERY_HEADS // KEY_VALUE_HEADS, HEAD_SIZE
    )
    token_key = local_entries[:, :key_value_width].reshape(entry_count, KEY_VALUE_HEADS, HEAD_SIZE)
    token_value = (
        local_entries[:, key_value_width:]
        .reshape(entry_count, KEY_VALUE_HEADS, HEAD_SIZE)
        .astype(jnp.float32)
    )
    own_score = jnp.einsum(
        "rhgd,rhd->rhg", query_vector, token_key, preferred_element_type=jnp.float32
    ) * (1.0 / math.sqrt(HEAD_SIZE))
    joined = jnp.maximum(maxima, own_score)
    old_coef = jnp.exp(maxima - joined)
    own_weight = jnp.exp(own_score - joined)
    totals = totals * old_coef + own_weight
    accum = accum * old_coef[..., None] + own_weight[..., None] * token_value[:, :, None, :]
    return (
        (accum / totals[..., None])
        .reshape(entry_count, QUERY_HEADS * HEAD_SIZE)
        .astype(jnp.bfloat16)
    )


def local_parts(query_all, paged_store_cache, page_table, cache_length, my_index):
    request_page_count = paged_store_cache.shape[0]
    page_length = paged_store_cache.shape[2]
    longest = page_table.shape[1]
    query_groups = QUERY_HEADS // KEY_VALUE_HEADS
    global_ids = my_index * request_page_count + jnp.arange(request_page_count, dtype=jnp.int32)
    matched = page_table[None, :, :] == global_ids[:, None, None]
    owner = jnp.any(matched, axis=2)
    position = jnp.sum(
        jnp.where(matched, jnp.arange(longest, dtype=jnp.int32)[None, None, :], 0), axis=(1, 2)
    )
    length_here = jnp.sum(jnp.where(owner, cache_length[None, :], 0), axis=1)
    query_page_scores = jnp.dot(
        owner.astype(jnp.bfloat16), query_all, preferred_element_type=jnp.float32
    ).astype(jnp.bfloat16)
    query_page_scores = query_page_scores.reshape(
        request_page_count, KEY_VALUE_HEADS, query_groups, HEAD_SIZE
    )
    key_matrix = paged_store_cache[:, 0].reshape(
        request_page_count, page_length, KEY_VALUE_HEADS, HEAD_SIZE
    )
    value_matrix = (
        paged_store_cache[:, 1]
        .reshape(request_page_count, page_length, KEY_VALUE_HEADS, HEAD_SIZE)
        .astype(jnp.float32)
    )
    scores = jnp.einsum(
        "phgd,pthd->phgt", query_page_scores, key_matrix, preferred_element_type=jnp.float32
    ) * (1.0 / math.sqrt(HEAD_SIZE))
    offsets = jnp.arange(page_length, dtype=jnp.int32)
    valid = position[:, None] * page_length + offsets[None, :] < length_here[:, None]
    scores = jnp.where(valid[:, None, None, :], scores, NEG_FILL)
    page_max = jnp.max(scores, axis=-1)
    weights = jnp.exp(scores - page_max[..., None])
    page_total = jnp.sum(weights, axis=-1)
    page_accum = jnp.einsum("phgt,pthd->phgd", weights, value_matrix)
    owned = owner[:, :, None, None]
    request_max = jnp.max(jnp.where(owned, page_max[:, None], NEG_FILL), axis=0)
    coef = jnp.where(owned, jnp.exp(page_max[:, None] - request_max[None]), 0.0)
    request_total = jnp.sum(coef * page_total[:, None], axis=0)
    request_accum = jnp.einsum("prhg,phgd->rhgd", coef, page_accum)
    return (request_max, request_total, request_accum)


def local(
    stream,
    queries,
    fresh_entries,
    paged_store_cache,
    page_table,
    cache_length,
    out_proj,
    norm_gain,
    router,
    routes,
    gate_up,
    down_proj,
):
    tensor_count = lax.axis_size("tensor")
    my_index = lax.axis_index("tensor")
    dec_rows = queries.shape[0]
    query_all, entries_all = (
        lax.all_gather(queries, "tensor", axis=0, tiled=True),
        lax.all_gather(fresh_entries, "tensor", axis=0, tiled=True),
    )
    request_max, request_total, request_accum = local_parts(
        query_all, paged_store_cache, page_table, cache_length, my_index
    )
    maxima = lax.pmax(request_max, "tensor")
    rescale = jnp.exp(request_max - maxima)
    totals, accum = lax.psum(
        (request_total * rescale, request_accum * rescale[..., None]), "tensor"
    )
    context = finish_context(maxima, totals, accum, query_all, entries_all)
    projected = jnp.dot(context, out_proj, preferred_element_type=jnp.float32)
    column_block = projected.shape[1]
    arrived = lax.all_to_all(
        projected.reshape(tensor_count, dec_rows, column_block),
        "tensor",
        split_axis=0,
        concat_axis=2,
        tiled=True,
    )
    widened = stream.astype(jnp.float32)
    widened = widened.at[:dec_rows].add(arrived[0])
    resid = lax.optimization_barrier(widened.astype(jnp.bfloat16))
    widened = resid.astype(jnp.float32)
    inverse = lax.rsqrt(jnp.mean(widened * widened, axis=-1, keepdims=True) + EPSILON)
    normed = (widened * inverse * norm_gain.astype(jnp.float32)).astype(jnp.bfloat16)
    logits = jnp.dot(normed, router, preferred_element_type=jnp.float32)
    chosen = jnp.take_along_axis(logits, routes, axis=1)
    gate_probs = jax.nn.softmax(chosen, axis=-1)
    expert_count = tensor_count // GROUP
    expert_ids = jnp.arange(expert_count, dtype=jnp.int32)
    matched = routes[:, :, None] == expert_ids[None, None, :]
    routed = jnp.any(matched, axis=1)
    gate_weight = jnp.sum(jnp.where(matched, gate_probs[:, :, None], 0.0), axis=1)
    routed_count = routed.astype(jnp.int32)
    ranking = jnp.cumsum(routed_count, axis=0) - routed_count
    slot_ids = jnp.arange(CAP, dtype=jnp.int32)
    selector = routed.T[:, None, :] & (ranking.T[:, None, :] == slot_ids[None, :, None])
    slot_rows = jnp.einsum(
        "eci,id->ecd", selector.astype(jnp.bfloat16), normed, preferred_element_type=jnp.float32
    ).astype(jnp.bfloat16)
    outgoing = jnp.repeat(slot_rows, GROUP, axis=0)
    contract_last = (((1,), (1,)), ((), ()))
    incoming = lax.all_to_all(outgoing, "tensor", split_axis=0, concat_axis=0, tiled=True)
    shape_in = incoming.shape
    flat_rows = incoming.reshape(-1, shape_in[2])
    gate_part = lax.dot_general(
        flat_rows, gate_up[0], contract_last, preferred_element_type=jnp.float32
    )
    upward = lax.dot_general(
        flat_rows, gate_up[1], contract_last, preferred_element_type=jnp.float32
    )
    active = (jax.nn.silu(gate_part) * upward).astype(jnp.bfloat16)
    partial_value = jnp.dot(active, down_proj, preferred_element_type=jnp.float32).astype(
        jnp.bfloat16
    )
    returned = lax.all_to_all(
        partial_value.reshape(shape_in), "tensor", split_axis=0, concat_axis=0, tiled=True
    )
    expert_out = jnp.sum(
        returned.reshape(expert_count, GROUP, CAP, returned.shape[2]), axis=1, dtype=jnp.float32
    )
    weighted = selector.astype(jnp.float32) * gate_weight.T[:, None, :]
    routed_sum = jnp.einsum("eci,ecd->id", weighted, expert_out)
    return (widened + routed_sum).astype(jnp.bfloat16)


def solution(mesh):
    placed = (
        P(("dp", "tensor"), None),
        P(("dp", "tensor"), None),
        P(("dp", "tensor"), None),
        P(("dp", "tensor"), None, None, None),
        P("dp", None),
        P("dp"),
        P(None, "tensor"),
        P(),
        P(),
        P(("dp", "tensor"), None),
        P(None, "tensor", None),
        P("tensor", None),
    )
    return jax.shard_map(
        local, mesh=mesh, in_specs=placed, out_specs=P(("dp", "tensor"), None), check_vma=False
    )
```

profile of v0, /device:TPU:40, one launch (start us, length us, event | category | flops | bytes accessed | tf_op | source)
XLA Modules:
  0.0 1744.6 jit_solution(13407701293075123612)
XLA Ops:
  6.5 1.1 fusion.28
  8.4 106.0 %all-gather = bf16[128,1,2560]{2,1,0:T(2,128)(2,1)S(1)} all-gather(bf16[1,1,2560]{2,1,0:T(2,128)(2,1)} %bitcast.71), channel_id=1, replica_groups=mesh['dp'=4,'tensor'=128] {'tensor'}, dimensions={0}, use_global_device_ids=true | all-gather | bytes 660480 | tf_op jit(solution)/shard_map/all_gather | solution.py:105
  115.5 2.3 fusion.59
  117.8 2.2 copy.144
  119.9 1.1 copy.143
  121.1 1.4 fusion.60
  122.9 1.6 fusion.31
  124.7 419.6 %pmax.7 = f32[128,4,5]{0,2,1:T(8,128)S(1)} all-reduce(f32[128,4,5]{0,2,1:T(8,128)S(1)} %select_reduce_fusion), channel_id=1, replica_groups=mesh['dp'=4,'tensor'=128] {'tensor'}, use_global_device_ids=true, to_apply=%region_5.6 | all-reduce | flops 2560 | bytes 20480 | tf_op jit(solution)/shard_map/pmax | solution.py:111
  544.4 1.5 fusion.2
  546.0 153.4 %all-gather.1 = bf16[128,1,1024]{2,1,0:T(2,128)(2,1)S(1)} all-gather(bf16[1,1,1024]{2,1,0:T(2,128)(2,1)S(1)} %bitcast.72), channel_id=1, replica_groups=mesh['dp'=4,'tensor'=128] {'tensor'}, dimensions={0}, use_global_device_ids=true | all-gather | bytes 264192 | tf_op jit(solution)/shard_map/all_gather | solution.py:106
  701.1 420.0 %psum.15 = f32[128,4,5]{0,2,1:T(8,128)S(1)} all-reduce(f32[128,4,5]{0,2,1:T(8,128)S(1)} %get-tuple-element.20), channel_id=1, replica_groups=mesh['dp'=4,'tensor'=128] {'tensor'}, use_global_device_ids=true, to_apply=%region_9.10 | all-reduce | flops 2560 | bytes 20480 | tf_op jit(solution)/shard_map/psum | solution.py:113
  1121.3 1.6 divide_convert_fusion
  1123.9 81.8 %all-to-all-start = ((f32[128,1,20]{2,1,0:T(1,128)}), f32[128,1,20]{2,1,0:T(1,128)S(1)}, u32[]{:S(2)}, u32[]{:S(2)}) async-start(f32[128,1,20]{2,1,0:T(1,128)} %bitcast.25), calls=%async_computation | async-start | bytes 131072 | tf_op jit(solution)/shard_map/all_to_all | solution.py:119
  1205.8 13.6 all-to-all-done
  1222.3 243.3 %all_to_all.19 = bf16[128,6,2560]{2,1,0:T(8,128)(2,1)} all-to-all(bf16[128,6,2560]{2,1,0:T(8,128)(2,1)S(1)} %bitcast.61), channel_id=1, replica_groups=mesh['dp'=4,'tensor'=128] {'tensor'}, dimensions={0} | all-to-all | bytes 7864320 | tf_op jit(solution)/shard_map/all_to_all | solution.py:149
  1465.7 7.3 reshape.163
  1472.9 3.8 fusion.7
  1476.7 7.5 convolution_convert_fusion
  1484.2 7.1 reshape.164
  1491.3 7.9 all-to-all-start.2
  1499.8 2.9 gather_fusion
  1503.0 230.2 %all-to-all-done.2 = bf16[128,6,2560]{2,1,0:T(8,128)(2,1)} async-done(((bf16[128,6,2560]{2,1,0:T(8,128)(2,1)}), bf16[128,6,2560]{2,1,0:T(8,128)(2,1)}, u32[]{:S(2)}, u32[]{:S(2)}) %all-to-all-start.2) | async-done | bytes 3932192 | tf_op jit(solution)/shard_map/all_to_all | solution.py:162
  1733.2 3.5 convert_reduce_fusion
  1736.7 1.0 fusion.1
  (68 shorter events, 9.3 us)
Async XLA Ops:
  6.5 1470.2 %copy-start = (bf16[192,2560]{1,0:T(8,128)(2,1)S(1)}, bf16[192,2560]{1,0:T(8,128)(2,1)}, u32[]{:S(2)}) copy-start(bf16[192,2560]{1,0:T(8,128)(2,1)} %param.25) | copy-start | bytes 2949124
  6.5 1114.7 %all-reduce.2.cloned.1.call-start = ((), (), s32[]{:S(2)}) async-start(), calls=%async_computation.3 | async-start | bytes 2621440 | tf_op jit(solution)/shard_map/psum | solution.py:113
  122.5 423.5 %copy-start.2 = (s32[64,6]{0,1:T(8,128)S(1)}, s32[64,6]{0,1:T(8,128)}, u32[]{:S(2)}) copy-start(s32[64,6]{0,1:T(8,128)} %param.23) | copy-start | bytes 4612
  122.5 423.5 %copy-start.5 = (bf16[1,1024]{1,0:T(2,128)(2,1)S(1)}, bf16[1,1024]{1,0:T(2,128)(2,1)}, u32[]{:S(2)}) copy-start(bf16[1,1024]{1,0:T(2,128)(2,1)} %param.16) | copy-start | bytes 6148
  700.9 421.9 %copy-start.3 = (bf16[2560,20]{0,1:T(8,128)(2,1)S(1)}, bf16[2560,20]{0,1:T(8,128)(2,1)}, u32[]{:S(2)}) copy-start(bf16[2560,20]{0,1:T(8,128)(2,1)} %param.20) | copy-start | bytes 307204
  1121.1 84.6 %copy-start.4 = (bf16[2560]{0:T(1024)(128)(2,1)S(1)}, bf16[2560]{0:T(1024)(128)(2,1)}, u32[]{:S(2)}) copy-start(bf16[2560]{0:T(1024)(128)(2,1)} %param.21) | copy-start | bytes 15364
  1121.1 84.6 %copy-start.1 = (bf16[64,2560]{1,0:T(8,128)(2,1)S(1)}, bf16[64,2560]{1,0:T(8,128)(2,1)}, u32[]{:S(2)}) copy-start(bf16[64,2560]{1,0:T(8,128)(2,1)} %param.14) | copy-start | bytes 983044
  1123.9 95.5 %all-to-all-start = ((f32[128,1,20]{2,1,0:T(1,128)}), f32[128,1,20]{2,1,0:T(1,128)S(1)}, u32[]{:S(2)}, u32[]{:S(2)}) async-start(f32[128,1,20]{2,1,0:T(1,128)} %bitcast.25), calls=%async_computation | async-start | bytes 131072 | tf_op jit(solution)/shard_map/all_to_all | solution.py:119
  1491.3 8.2 copy-start.6
  1491.3 241.9 %all-to-all-start.2 = ((bf16[128,6,2560]{2,1,0:T(8,128)(2,1)}), bf16[128,6,2560]{2,1,0:T(8,128)(2,1)}, u32[]{:S(2)}, u32[]{:S(2)}) async-start(bf16[128,6,2560]{2,1,0:T(8,128)(2,1)} %reshape.164), calls=%async_computation.2 | async-start | bytes 10485760 | tf_op jit(solution)/shard_map/all_to_all | solution.py:162
Sparse Core Ops, SparseCore 0:
  546.1 408.8 all-reduce.1
where the time goes:
time: 1750 us; the launch traced here: 1740 us
  blocking collectives  1340 us (77%)
  waiting for transfers between devices  244 us (14%)
  starting transfers between devices  89.7 us (5%)
  local copies, waits for them, and re-layouts  26.5 us (2%)
  matrix products  18.7 us (1%)
    psum x1, blocking collectives, local(): lax.psum((request_total * rescale, request_accum * rescale[..., None]), '...  420 us
    pmax x1, blocking collectives, local(): maxima = lax.pmax(request_max, 'tensor')  420 us
    all_to_all x1, blocking collectives, local(): lax.all_to_all(outgoing, 'tensor', split_axis=0, concat_axis=0, tiled=True)  243 us
    all_to_all x1, waiting for transfers between devices, local(): lax.all_to_all(partial_value.reshape(shape_in), 'tensor', split_axis=0, c...  230 us
    all_gather x1, blocking collectives, local(): lax.all_gather(fresh_entries, 'tensor', axis=0, tiled=True)  153 us
    all_gather x1, blocking collectives, local(): lax.all_gather(queries, 'tensor', axis=0, tiled=True)  106 us
    all_to_all x1, starting transfers between devices, local(): lax.all_to_all(projected.reshape(tensor_count, dec_rows, column_block), '...  81.8 us
  transfers between devices with their start and end apart: 3, of which 2 were waited for; matrix products, arithmetic and copies ran while one was open for 0% of the time, Pallas kernels for 0%

commit v1 on v0

--- a/solution.py
+++ b/solution.py
@@ -103,7 +103,10 @@
     dec_rows = queries.shape[0]
     query_all, entries_all = (
         lax.all_gather(queries, "tensor", axis=0, tiled=True),
-        lax.all_gather(fresh_entries, "tensor", axis=0, tiled=True),
+        jnp.concatenate(
+            lax.all_to_all(jnp.stack([fresh_entries] * lax.axis_size("tensor")), "tensor", 0, 0),
+            axis=0,
+        ),
     )
     request_max, request_total, request_accum = local_parts(
         query_all, paged_store_cache, page_table, cache_length, my_index

time: 1750 us -> 1690 us (0.966)
  blocking collectives: 1340 us -> 1260 us
  starting transfers between devices: 89.7 us -> 109 us
    all_gather x1 -> x0, blocking collectives: 153 us -> none  [local(): lax.all_gather(fresh_entries, 'tensor', axis=0, tiled=True)]
    psum x1, blocking collectives: 420 us -> 491 us  [local(): lax.psum((request_total * rescale, request_accum * rescale[..., None]), '...]
    all_to_all x0 -> x1, starting transfers between devices: none -> 19.2 us  [local(): lax.all_to_all(jnp.stack([fresh_entries] * lax.axis_size('tensor')), 'ten...]
  transfers between devices with their start and end apart: 3 -> 4, of which waited for: 2 -> 2; matrix products, arithmetic and copies ran while one was open for 0% -> 1% of each run, Pallas kernels for 0% -> 0%
where the time goes in v1:
time: 1690 us; the launch traced here: 1680 us
  blocking collectives  1260 us (75%)
  waiting for transfers between devices  244 us (14%)
  starting transfers between devices  109 us (6%)
  local copies, waits for them, and re-layouts  28.4 us (2%)
  matrix products  18.7 us (1%)
    psum x1, blocking collectives, local(): lax.psum((request_total * rescale, request_accum * rescale[..., None]), '...  491 us
    pmax x1, blocking collectives, local(): maxima = lax.pmax(request_max, 'tensor')  418 us
    all_to_all x1, blocking collectives, local(): lax.all_to_all(outgoing, 'tensor', split_axis=0, concat_axis=0, tiled=True)  243 us
    all_to_all x1, waiting for transfers between devices, local(): lax.all_to_all(partial_value.reshape(shape_in), 'tensor', split_axis=0, c...  230 us
    all_gather x1, blocking collectives, local(): lax.all_gather(queries, 'tensor', axis=0, tiled=True)  108 us
    all_to_all x1, starting transfers between devices, local(): lax.all_to_all(projected.reshape(tensor_count, dec_rows, column_block), '...  81.6 us
  transfers between devices with their start and end apart: 4, of which 2 were waited for; matrix products, arithmetic and copies ran while one was open for 1% of the time, Pallas kernels for 0%

profile of v1, /device:TPU:40, one launch (start us, length us, event | category | flops | bytes accessed | tf_op | source)
XLA Modules:
  0.0 1684.7 jit_solution(8332447780211166732)
XLA Ops:
  8.1 2.1 reduce.9
  11.2 19.2 %all-to-all-start = ((bf16[128,2,512]{2,1,0:T(2,128)(2,1)}), bf16[128,2,512]{2,1,0:T(2,128)(2,1)S(1)}, u32[]{:S(2)}, u32[]{:S(2)}) async-start(bf16[128,2,512]{2,1,0:T(2,128)(2,1)} %reshape.202), calls=%async_computation | async-start | bytes 524288 | tf_op jit(solution)/shard_map/all_to_all | solution.py:107
  30.8 107.7 %all-gather = bf16[128,1,2560]{2,1,0:T(2,128)(2,1)S(1)} all-gather(bf16[1,1,2560]{2,1,0:T(2,128)(2,1)S(1)} %bitcast.70), channel_id=1, replica_groups=mesh['dp'=4,'tensor'=128] {'tensor'}, dimensions={0}, use_global_device_ids=true | all-gather | bytes 660480 | tf_op jit(solution)/shard_map/all_gather | solution.py:105
  138.9 2.3 fusion.59
  141.1 2.2 copy.126
  143.3 1.1 copy.125
  144.5 1.4 fusion.60
  146.5 418.4 %pmax.7 = f32[128,4,5]{0,2,1:T(8,128)S(1)} all-reduce(f32[128,4,5]{0,2,1:T(8,128)S(1)} %select_reduce_fusion), channel_id=1, replica_groups=mesh['dp'=4,'tensor'=128] {'tensor'}, use_global_device_ids=true, to_apply=%region_5.6 | all-reduce | flops 2560 | bytes 20480 | tf_op jit(solution)/shard_map/pmax | solution.py:114
  565.0 1.6 fusion.31
  566.6 1.6 fusion.2
  569.4 491.2 %psum.15 = f32[128,4,5]{0,2,1:T(8,128)S(1)} all-reduce(f32[128,4,5]{0,2,1:T(8,128)S(1)} %get-tuple-element.20), channel_id=1, replica_groups=mesh['dp'=4,'tensor'=128] {'tensor'}, use_global_device_ids=true, to_apply=%region_9.10 | all-reduce | flops 2560 | bytes 20480 | tf_op jit(solution)/shard_map/psum | solution.py:116
  1061.6 1.6 divide_convert_fusion
  1064.2 81.6 %all-to-all-start.1 = ((f32[128,1,20]{2,1,0:T(1,128)}), f32[128,1,20]{2,1,0:T(1,128)S(1)}, u32[]{:S(2)}, u32[]{:S(2)}) async-start(f32[128,1,20]{2,1,0:T(1,128)} %bitcast.24), calls=%async_computation.1 | async-start | bytes 131072 | tf_op jit(solution)/shard_map/all_to_all | solution.py:122
  1145.9 13.6 all-to-all-done.1
  1162.4 243.3 %all_to_all.24 = bf16[128,6,2560]{2,1,0:T(8,128)(2,1)} all-to-all(bf16[128,6,2560]{2,1,0:T(8,128)(2,1)S(1)} %bitcast.60), channel_id=1, replica_groups=mesh['dp'=4,'tensor'=128] {'tensor'}, dimensions={0} | all-to-all | bytes 7864320 | tf_op jit(solution)/shard_map/all_to_all | solution.py:152
  1405.8 7.3 reshape.170
  1413.0 3.8 fusion.7
  1416.8 7.5 convolution_convert_fusion
  1424.3 7.1 reshape.171
  1431.4 7.9 all-to-all-start.3
  1439.9 2.9 gather_fusion
  1443.1 230.2 %all-to-all-done.3 = bf16[128,6,2560]{2,1,0:T(8,128)(2,1)} async-done(((bf16[128,6,2560]{2,1,0:T(8,128)(2,1)}), bf16[128,6,2560]{2,1,0:T(8,128)(2,1)}, u32[]{:S(2)}, u32[]{:S(2)}) %all-to-all-start.3) | async-done | bytes 3932192 | tf_op jit(solution)/shard_map/all_to_all | solution.py:165
  1673.3 3.5 convert_reduce_fusion
  1676.8 1.0 fusion.1
  (79 shorter events, 10.9 us)
Async XLA Ops:
  6.5 1410.3 %copy-start = (bf16[192,2560]{1,0:T(8,128)(2,1)S(1)}, bf16[192,2560]{1,0:T(8,128)(2,1)}, u32[]{:S(2)}) copy-start(bf16[192,2560]{1,0:T(8,128)(2,1)} %param.25) | copy-start | bytes 2949124
  6.5 23.9 %copy-start.4 = (s32[128,32]{0,1:T(8,128)S(1)}, s32[128,32]{0,1:T(8,128)}, u32[]{:S(2)}) copy-start(s32[128,32]{0,1:T(8,128)} %param.18) | copy-start | bytes 49156
  6.5 24.3 %copy-start.5 = (bf16[1,2560]{1,0:T(2,128)(2,1)S(1)}, bf16[1,2560]{1,0:T(2,128)(2,1)}, u32[]{:S(2)}) copy-start(bf16[1,2560]{1,0:T(2,128)(2,1)} %param.15) | copy-start | bytes 15364
  6.5 132.0 %copy-start.7 = (s32[128]{0:T(128)S(1)}, s32[128]{0:T(128)}, u32[]{:S(2)}) copy-start(s32[128]{0:T(128)} %param.19) | copy-start | bytes 1540
  11.2 1049.5 %all-to-all-start = ((bf16[128,2,512]{2,1,0:T(2,128)(2,1)}), bf16[128,2,512]{2,1,0:T(2,128)(2,1)S(1)}, u32[]{:S(2)}, u32[]{:S(2)}) async-start(bf16[128,2,512]{2,1,0:T(2,128)(2,1)} %reshape.202), calls=%async_computation | async-start | bytes 524288 | tf_op jit(solution)/shard_map/all_to_all | solution.py:107
  30.3 1031.2 %all-reduce.2.cloned.1.call-start = ((), (), s32[]{:S(2)}) async-start(), calls=%async_computation.4 | async-start | bytes 2621440 | tf_op jit(solution)/shard_map/psum | solution.py:116
  145.9 422.3 %copy-start.2 = (s32[64,6]{0,1:T(8,128)S(1)}, s32[64,6]{0,1:T(8,128)}, u32[]{:S(2)}) copy-start(s32[64,6]{0,1:T(8,128)} %param.23) | copy-start | bytes 4612
  1061.1 2.0 copy-start.3
  1061.3 84.5 %copy-start.6 = (bf16[2560]{0:T(1024)(128)(2,1)S(1)}, bf16[2560]{0:T(1024)(128)(2,1)}, u32[]{:S(2)}) copy-start(bf16[2560]{0:T(1024)(128)(2,1)} %param.21) | copy-start | bytes 15364
  1061.3 84.5 %copy-start.1 = (bf16[64,2560]{1,0:T(8,128)(2,1)S(1)}, bf16[64,2560]{1,0:T(8,128)(2,1)}, u32[]{:S(2)}) copy-start(bf16[64,2560]{1,0:T(8,128)(2,1)} %param.14) | copy-start | bytes 983044
  1064.2 95.3 %all-to-all-start.1 = ((f32[128,1,20]{2,1,0:T(1,128)}), f32[128,1,20]{2,1,0:T(1,128)S(1)}, u32[]{:S(2)}, u32[]{:S(2)}) async-start(f32[128,1,20]{2,1,0:T(1,128)} %bitcast.24), calls=%async_computation.1 | async-start | bytes 131072 | tf_op jit(solution)/shard_map/all_to_all | solution.py:122
  1431.4 8.2 copy-start.8
  1431.4 241.9 %all-to-all-start.3 = ((bf16[128,6,2560]{2,1,0:T(8,128)(2,1)}), bf16[128,6,2560]{2,1,0:T(8,128)(2,1)}, u32[]{:S(2)}, u32[]{:S(2)}) async-start(bf16[128,6,2560]{2,1,0:T(8,128)(2,1)} %reshape.171), calls=%async_computation.3 | async-start | bytes 10485760 | tf_op jit(solution)/shard_map/all_to_all | solution.py:165
Sparse Core Ops, SparseCore 0:
  568.3 407.9 all-reduce.1
